TPU v7x, 512 devices: a whole 4x8x8 slice. The times are simulated.
512 devices in a mesh: depth: 16 (over z_lo, x, core), height: 8 (over y), sample: 4 (over z_hi).
Axes of the slice: x: 4, y: 8, z: 8 (z_hi: 4, z_lo: 2; z = z_hi * 2 + z_lo), core: 2. Of those that a mesh axis runs over, the one named last changes fastest.
Arguments:
- volume: bfloat16 [4, 4, 64, 32, 512], P('sample', None, 'depth', 'height'), may hold values from -6 to 6
- kernel_one: bfloat16 [32, 108], replicated, may hold values from -0.625 to 0.625
- kernel_two: bfloat16 [64, 864], P('height'), may hold values from -0.21875 to 0.21875
- cotangent: bfloat16 [4, 64, 16, 1024], P('sample', 'height', 'depth'), may hold values from -24 to 24
Outputs:
- pooled_two: bfloat16 [4, 64, 16, 1024], P('sample', 'height', 'depth')
- weight_grad: float32 [64, 864], P('height')
- act_grad: bfloat16 [4, 32, 32, 16, 256], P('sample', None, 'depth', 'height')
All inputs are finite; a program needn't handle non-finite values.
Results may differ from a plain program's by a relative error of at most 0.005.
Values may be sent and summed in bfloat16 or wider, within the bound.
No kernel may reach another device: no remote copies, remote signals or barrier semaphores. Data moves between devices by JAX's collectives and lax.ppermute only.
A program may use at most 64 MiB of HBM per device.

v0:
```python
import jax
import jax.numpy as jnp
from jax import lax
from jax.sharding import PartitionSpec as P

LEAK_SLOPE = 0.3
CONV_DIMS = ("NCDHW", "OIDHW", "NCDHW")


def extended(block, sides, width):
    for axis, dim in sides:
        count = lax.axis_size(axis)
        forward = [(i, i + 1) for i in range(count - 1)]
        backward = [(target, source) for source, target in forward]
        low = lax.ppermute(
            lax.slice_in_dim(block, block.shape[dim] - width, None, axis=dim), axis, forward
        )
        high = lax.ppermute(lax.slice_in_dim(block, 0, width, axis=dim), axis, backward)
        block = jnp.concatenate([low, block, high], axis=dim)
    return block


def butterfly_sum(values, axes):
    sizes = [lax.axis_size(axis) for axis in axes]
    count = 1
    for size in sizes:
        count *= size
    if count & count - 1:
        return lax.psum(values, axes)
    inner = lax.axis_size(axes[-1])

    def label(i):
        low = i % inner
        i = i - low + (low ^ low >> 1)
        mid = i // (inner * 2) % 4
        return i + ((mid ^ mid >> 1) - mid) * inner * 2

    owner = {label(i): i for i in range(count)}
    step = 1
    while step < count:
        pairs = [(i, owner[label(i) ^ step]) for i in range(count)]
        values = values + lax.ppermute(values, axes, pairs)
        step *= 2
    return values


def halving_scatter(values, axis, dim):
    count = lax.axis_size(axis)
    if count & count - 1:
        return lax.psum_scatter(values, axis, scatter_dimension=dim, tiled=True)
    index = lax.axis_index(axis)
    step = count // 2
    while step >= 1:
        half = values.shape[dim] // 2
        bit = index // step % 2
        keep = lax.dynamic_slice_in_dim(values, bit * half, half, axis=dim)
        send = lax.dynamic_slice_in_dim(values, (1 - bit) * half, half, axis=dim)
        pairs = [(i, i ^ step) for i in range(count)]
        values = keep + lax.ppermute(send, axis, pairs)
        step //= 2
    return values


def delta_shifts(delta_ext):
    _, _, _, hsize, wsize = delta_ext.shape
    dpad = jnp.pad(delta_ext[0], ((0, 0), (0, 0), (1, 1), (1, 1)))
    return jnp.stack(
        [
            dpad[:, :, 2 - kh : 2 - kh + hsize, 2 - kw : 2 - kw + wsize]
            for kh in range(3)
            for kw in range(3)
        ],
        axis=1,
    )


def weight_gradient(level_ext, shifted):
    chans = level_ext.shape[1]
    filters, _, dsize, _, _ = shifted.shape
    levels = jnp.stack([level_ext[0, :, kd : kd + dsize] for kd in range(3)], axis=0)
    grad = lax.dot_general(
        shifted, levels, (((2, 3, 4), (2, 3, 4)), ((), ())), preferred_element_type=jnp.float32
    )
    grad = grad.reshape(filters, 3, 3, 3, chans)
    return jnp.transpose(grad, (0, 4, 3, 1, 2)).reshape(filters, chans * 27)


def back_product(shifts_ext, kernel):
    filters, chans = kernel.shape[:2]
    dsize = shifts_ext.shape[2] - 2
    stacked = jnp.stack([shifts_ext[:, :, 2 - kd : 2 - kd + dsize] for kd in range(3)], axis=0)
    weights = jnp.transpose(kernel, (1, 2, 0, 3, 4)).reshape(chans, 3, filters, 9)
    grad = lax.dot_general(
        weights, stacked, (((1, 2, 3), (0, 1, 2)), ((), ())), preferred_element_type=jnp.float32
    )
    return grad[None]


def forward_product(level_ext, kernel):
    filters, chans = kernel.shape[:2]
    dsize = level_ext.shape[2] - 2
    shifts = delta_shifts(level_ext)
    stacked = jnp.stack([shifts[:, :, kd : kd + dsize] for kd in range(3)], axis=0)
    flipped = jnp.flip(kernel, axis=(3, 4))
    weights = jnp.transpose(flipped, (0, 2, 1, 3, 4)).reshape(filters, 3, chans, 9)
    grad = lax.dot_general(
        weights, stacked, (((1, 2, 3), (0, 1, 2)), ((), ())), preferred_element_type=jnp.float32
    )
    return grad[None]


def near_first_scatter(values, axis):
    count = lax.axis_size(axis)
    chans, dsize, hsize, wsize = values.shape[1:]
    if count & count - 1:
        return lax.psum_scatter(values, axis, scatter_dimension=3, tiled=True)
    bits = count.bit_length() - 1
    rows = hsize // count
    index = lax.axis_index(axis)
    grid = jnp.transpose(values[0], (2, 1, 0, 3))
    grid = grid.reshape((2,) * bits + (rows, dsize, chans, wsize))
    for t in range(bits):
        axis_pos = bits - 1 - t
        bit = index >> t & 1
        keep = lax.dynamic_slice_in_dim(grid, bit, 1, axis=axis_pos)
        send = lax.dynamic_slice_in_dim(grid, 1 - bit, 1, axis=axis_pos)
        pairs = [(i, i ^ 1 << t) for i in range(count)]
        grid = jnp.squeeze(keep + lax.ppermute(send, axis, pairs), axis_pos)
    return jnp.transpose(grid, (2, 1, 0, 3))[None]


def activate(values):
    return LEAK_SLOPE * values + (1.0 - LEAK_SLOPE) * jax.nn.softplus(values)


def slope_at(values):
    return LEAK_SLOPE + (1.0 - LEAK_SLOPE) * jax.nn.sigmoid(values)


def pooled(values):
    count, chans, dsize, hsize, wsize = values.shape
    blocks = values.reshape(count, chans, dsize // 2, 2, hsize // 2, 2, wsize // 2, 2)
    return blocks.mean(axis=(3, 5, 7))


def spread_up(values):
    values = jnp.repeat(jnp.repeat(jnp.repeat(values, 2, axis=2), 2, axis=3), 2, axis=4)
    return values * 0.125


def conv_valid(inputs, kernel):
    return lax.conv_general_dilated(
        inputs,
        kernel,
        (1, 1, 1),
        "VALID",
        dimension_numbers=CONV_DIMS,
        preferred_element_type=jnp.float32,
    )


def back_conv(delta_pad, kernel):
    flipped = jnp.flip(kernel, axis=(2, 3, 4))
    return lax.conv_general_dilated(
        delta_pad,
        flipped,
        (1, 1, 1),
        "VALID",
        dimension_numbers=("NCDHW", "IODHW", "NCDHW"),
        preferred_element_type=jnp.float32,
    )


def shards(volume, kernel_one, kernel_two, cotangent):
    depth_count = lax.axis_size("depth")
    height_count = lax.axis_size("height")
    sample_count = lax.axis_size("sample")
    chans_in = volume.shape[1]
    depth_loc = volume.shape[2]
    height_loc = volume.shape[3]
    width_all = volume.shape[4]
    chans_mid = kernel_one.shape[0]
    filters = kernel_two.shape[0]
    first_kernel = kernel_one.reshape(chans_mid, chans_in, 3, 3, 3)
    second_kernel = kernel_two.reshape(filters, chans_mid, 3, 3, 3)
    padded = extended(volume, (("depth", 2), ("height", 3)), 1)
    pre_one = forward_product(padded, first_kernel)[:, :, :, 1:-1]
    level_loc = pooled(activate(pre_one)).astype(jnp.bfloat16)
    slab_rows = lax.all_gather(level_loc, "height", axis=3, tiled=True)
    level_one = extended(slab_rows, (("depth", 2),), 1)
    pre_two = forward_product(level_one, second_kernel)
    pooled_grid = pooled(activate(pre_two)).astype(jnp.bfloat16)
    depth_two = pooled_grid.shape[2]
    pooled_two = pooled_grid.reshape(
        1, filters, depth_two, pooled_grid.shape[3] * pooled_grid.shape[4]
    )
    cot_grid = cotangent.reshape(1, filters, depth_two, pooled_grid.shape[3], pooled_grid.shape[4])
    delta_two = (spread_up(cot_grid.astype(jnp.float32)) * slope_at(pre_two)).astype(jnp.bfloat16)
    scale = (
        1.0
        / float(
            sample_count
            * (depth_loc // 2)
            * depth_count
            * (height_loc // 2)
            * height_count
            * (width_all // 2)
        )
        ** 0.5
    )
    delta_ext = extended(delta_two, (("depth", 2),), 1)
    shifts_ext = delta_shifts(delta_ext)
    weight_term = weight_gradient(level_one, delta_shifts(delta_two)) * scale
    flat_size = weight_term.size
    lanes = 128 if flat_size % 128 == 0 else flat_size
    weight_grad = butterfly_sum(
        weight_term.reshape(flat_size // lanes, lanes), ("depth", "sample")
    ).reshape(weight_term.shape)
    back_part = back_product(shifts_ext, second_kernel)
    act_grad = near_first_scatter(back_part, "height").astype(jnp.bfloat16)
    return (pooled_two, weight_grad, act_grad)


def solution(mesh):
    in_specs = (
        P("sample", None, "depth", "height", None),
        P(),
        P("height", None),
        P("sample", "height", "depth", None),
    )
    out_specs = (
        P("sample", "height", "depth", None),
        P("height", None),
        P("sample", None, "depth", "height", None),
    )
    return jax.shard_map(shards, mesh=mesh, in_specs=in_specs, out_specs=out_specs, check_vma=False)
```

profile of v0, /device:TPU:8, one launch (start us, length us, event | category | flops | bytes accessed | tf_op | source)
XLA Modules:
  0.0 182.4 jit_solution(10404301565494377352)
XLA Ops:
  1.4 1.7 collective-permute-start
  3.1 1.3 collective-permute-start.1
  4.5 0.9 constant_dynamic-update-slice_fusion.1
  5.3 2.2 %collective-permute-done.1 = bf16[1,4,1,4,512]{4,3,2,1,0:T(4,128)(2,1)S(1)} collective-permute-done((bf16[1,4,1,4,512]{4,3,2,1,0:T(4,128)(2,1)S(1)}, bf16[1,4,1,4,512]{4,3,2,1,0:T(4,128)(2,1)S(1)}, u32[]{:S(2)}, u32[]{:S(2)}) %collective-permute-start.1) | collective-permute-done | bytes 16416 | tf_op jit(solution)/shard_map/ppermute | solution.py:18
  7.6 3.5 %collective-permute-start.2 = (bf16[1,4,6,1,512]{4,3,2,1,0:T(2,128)(2,1)S(1)}, bf16[1,4,6,1,512]{4,3,2,1,0:T(2,128)(2,1)S(1)}, u32[]{:S(2)}, u32[]{:S(2)}) collective-permute-start(bf16[1,4,6,1,512]{4,3,2,1,0:T(2,128)(2,1)S(1)} %get-tuple-element.57), channel_id=1, source_target_pairs={{0,4},{4,8},{8,12},{12,16},{16,20},{20,24},{24,28},{1,5},{5,9},{9,... | collective-permute-start | bytes 73736 | tf_op jit(solution)/shard_map/ppermute | solution.py:15
  11.1 3.8 %collective-permute-start.3 = (bf16[1,4,6,1,512]{4,3,2,1,0:T(2,128)(2,1)S(1)}, bf16[1,4,6,1,512]{4,3,2,1,0:T(2,128)(2,1)S(1)}, u32[]{:S(2)}, u32[]{:S(2)}) collective-permute-start(bf16[1,4,6,1,512]{4,3,2,1,0:T(2,128)(2,1)S(1)} %get-tuple-element.58), channel_id=1, source_target_pairs={{4,0},{8,4},{12,8},{16,12},{20,16},{24,20},{28,24},{5,1},{9,5},{13... | collective-permute-start | bytes 73736 | tf_op jit(solution)/shard_map/ppermute | solution.py:18
  14.9 0.8 copy.389
  18.9 0.9 copy.383
  19.9 0.9 copy.384
  20.8 1.0 copy.385
  21.8 0.9 copy.386
  22.7 0.9 copy.382
  23.7 11.4 %stack.168 = bf16[4,9,6,6,512]{4,1,0,3,2:T(8,128)(2,1)S(1)} concatenate(bf16[4,1,6,6,512]{4,1,0,3,2:T(2,128)(2,1)S(1)} %copy.378, bf16[4,1,6,6,512]{4,1,0,3,2:T(2,128)(2,1)S(1)} %copy.379, bf16[4,1,6,6,512]{4,1,0,3,2:T(2,128)(2,1)S(1)} %copy.380, bf16[4,1,6,6,512]{4,1,0,3,2:T(2,128)(2,1)S(1)} %copy.381, bf16[4,1,6,6,512]{4,1,0,3,2:T(2,128)(2,1)} %copy.382, ...), dimensions={1} | concatenate | bytes 2654208 | tf_op jit(solution)/shard_map/stack | solution.py:67
  35.9 1.4 fusion.27
  37.9 2.6 %copy.392 = f32[1,32,4,4,512]{1,4,3,2,0:T(8,128)} copy(f32[1,32,4,4,512]{4,1,3,2,0:T(8,128)S(1)} %fusion.61) | data formatting | bytes 2097152 | tf_op jit(solution)/shard_map/add | solution.py:133
  40.5 4.8 %reduce_sum.21 = f32[32,2,2,256]{0,3,2,1:T(8,128)S(1)} reduce(f32[32,2,2,2,2,256,2]{0,6,5,4,3,2,1:T(2,128)} %bitcast.266, f32[]{:T(128)} %constant.17.clone.1), dimensions={2,4,6}, to_apply=%region_0.1 | reduce | flops 229376 | bytes 1179652 | tf_op jit(solution)/shard_map/reduce_sum | solution.py:143
  45.5 27.9 %all-gather = bf16[32,2,16,256]{3,0,2,1:T(8,128)(2,1)S(1)} all-gather(bf16[32,2,2,256]{3,0,2,1:T(8,128)(2,1)S(1)} %multiply_convert_fusion.2), channel_id=2, replica_groups=mesh['depth'=16,'height'=8,'sample'=4] {'height'}, dimensions={2}, use_global_device_ids=true | all-gather | bytes 589824 | tf_op jit(solution)/shard_map/all_gather | solution.py:189
  73.5 1.3 collective-permute-start.4
  74.8 1.5 collective-permute-start.5
  77.3 0.8 copy.405
  79.1 1.7 collective-permute-done.5
  83.8 2.8 %slice_bitcast_fusion.2 = (bf16[1,32,9,2,16,256]{5,1,2,0,4,3:T(8,128)(2,1)S(1)}, bf16[1,32,9,2,16,256]{5,1,2,0,4,3:T(8,128)(2,1)S(1)}, bf16[1,32,9,2,16,256]{5,1,2,0,4,3:T(8,128)(2,1)S(1)}) fusion(bf16[32,9,4,16,256]{4,0,1,3,2:T(8,128)(2,1)S(1)} %fusion.59), kind=kLoop, calls=%fused_computation.8 | loop fusion | bytes 28311552 | tf_op jit(solution)/shard_map/stack | solution.py:103
  86.5 2.6 %multiply_convert_fusion.1 = (bf16[8,2,16,256]{3,0,2,1:T(8,128)(2,1)S(1)}, f32[8,16,256]{2,0,1:T(8,128)S(1)}) fusion(f32[8,16,256]{2,0,1:T(8,128)S(1)} %copy.408, bf16[8,3,32,9,1,1]{2,0,3,1,5,4:T(8,128)(2,1)S(1)} %bitcast.281, bf16[1,32,9,2,16,256]{5,1,2,0,4,3:T(8,128)(2,1)S(1)} %get-tuple-element.31, ...), kind=kOutput, calls=%fused_computation.113 | convolution fusion | flops 128483328 | bytes 14562816 | tf_op jit(solution)/shard_map/dot_general | solution.py:106
  89.3 6.7 %collective-permute-start.12 = (bf16[1,8,1,16,256]{4,1,3,2,0:T(8,128)(2,1)S(1)}, bf16[1,8,1,16,256]{4,1,3,2,0:T(8,128)(2,1)S(1)}, u32[]{:S(2)}, u32[]{:S(2)}) collective-permute-start(bf16[1,8,1,16,256]{4,1,3,2,0:T(8,128)(2,1)S(1)} %get-tuple-element.55), channel_id=1, source_target_pairs={{0,32},{32,64},{64,96},{96,128},{128,160},{160,192},{192,224},{224... | collective-permute-start | bytes 196616 | tf_op jit(solution)/shard_map/ppermute | solution.py:15
  96.0 1.3 collective-permute-start.13
  97.6 1.6 collective-permute-done.13
  100.5 0.9 fusion.12
  101.6 1.9 %collective-permute-start.14 = (f32[2,2,1,2,2,32,256]{6,5,4,3,0,2,1:T(8,128)S(1)}, f32[2,2,1,2,2,32,256]{6,5,4,3,0,2,1:T(8,128)S(1)}, u32[]{:S(2)}, u32[]{:S(2)}) collective-permute-start(f32[2,2,1,2,2,32,256]{6,5,4,3,0,2,1:T(8,128)S(1)} %copy.444), channel_id=1, source_target_pairs={{0,4},{4,0},{8,12},{12,8},{16,20},{20,16},{24,28},{28,24},{1,5},{5... | collective-permute-start | bytes 1572872 | tf_op jit(solution)/shard_map/ppermute | solution.py:128
  103.9 12.7 %collective-permute-done.14 = f32[2,2,1,2,2,32,256]{6,5,4,3,0,2,1:T(8,128)S(1)} collective-permute-done((f32[2,2,1,2,2,32,256]{6,5,4,3,0,2,1:T(8,128)S(1)}, f32[2,2,1,2,2,32,256]{6,5,4,3,0,2,1:T(8,128)S(1)}, u32[]{:S(2)}, u32[]{:S(2)}) %collective-permute-start.14) | collective-permute-done | bytes 524320 | tf_op jit(solution)/shard_map/ppermute | solution.py:128
  116.7 4.6 %collective-permute-start.15 = (f32[2,1,2,2,32,256]{5,4,3,2,0,1:T(8,128)S(1)}, f32[2,1,2,2,32,256]{5,4,3,2,0,1:T(8,128)}, u32[]{:S(2)}, u32[]{:S(2)}) collective-permute-start(f32[2,1,2,2,32,256]{5,4,3,2,0,1:T(8,128)S(1)} %dynamic-slice_bitcast_fusion), channel_id=1, source_target_pairs={{0,8},{4,12},{8,0},{12,4},{16,24},{20,28},{24,16},{28,20},{1,9},{5... | collective-permute-start | bytes 786440 | tf_op jit(solution)/shard_map/ppermute | solution.py:128
  121.2 1.2 fusion.39
  122.5 1.2 copy.409
  123.7 1.0 mul.80
  124.7 6.1 %collective-permute-start.6 = (f32[54,128]{1,0:T(8,128)S(1)}, f32[54,128]{1,0:T(8,128)S(1)}, u32[]{:S(2)}, u32[]{:S(2)}) collective-permute-start(f32[54,128]{1,0:T(8,128)S(1)} %mul.80), channel_id=1, source_target_pairs={{0,1},{1,0},{2,3},{3,2},{32,33},{33,32},{34,35},{35,34},{64,65},{6... | collective-permute-start | bytes 82952 | tf_op jit(solution)/shard_map/ppermute | solution.py:42
  130.8 1.8 %collective-permute-done.6 = f32[54,128]{1,0:T(8,128)S(1)} collective-permute-done((f32[54,128]{1,0:T(8,128)S(1)}, f32[54,128]{1,0:T(8,128)S(1)}, u32[]{:S(2)}, u32[]{:S(2)}) %collective-permute-start.6) | collective-permute-done | bytes 27680 | tf_op jit(solution)/shard_map/ppermute | solution.py:42
  132.6 9.7 %collective-permute-start.7 = (f32[54,128]{1,0:T(8,128)S(1)}, f32[54,128]{1,0:T(8,128)S(1)}, u32[]{:S(2)}, u32[]{:S(2)}) collective-permute-start(f32[54,128]{1,0:T(8,128)S(1)} %add.86), channel_id=1, source_target_pairs={{0,3},{1,2},{2,1},{3,0},{32,35},{33,34},{34,33},{35,32},{64,67},{6... | collective-permute-start | bytes 82952 | tf_op jit(solution)/shard_map/ppermute | solution.py:42
  142.3 1.8 %collective-permute-done.7 = f32[54,128]{1,0:T(8,128)S(1)} collective-permute-done((f32[54,128]{1,0:T(8,128)S(1)}, f32[54,128]{1,0:T(8,128)S(1)}, u32[]{:S(2)}, u32[]{:S(2)}) %collective-permute-start.7) | collective-permute-done | bytes 27680 | tf_op jit(solution)/shard_map/ppermute | solution.py:42
  144.1 1.9 %collective-permute-start.8 = (f32[54,128]{1,0:T(8,128)S(1)}, f32[54,128]{1,0:T(8,128)S(1)}, u32[]{:S(2)}, u32[]{:S(2)}) collective-permute-start(f32[54,128]{1,0:T(8,128)S(1)} %add.87), channel_id=1, source_target_pairs={{0,32},{1,33},{2,34},{3,35},{32,0},{33,1},{34,2},{35,3},{64,96},{6... | collective-permute-start | bytes 82952 | tf_op jit(solution)/shard_map/ppermute | solution.py:42
  146.0 1.2 collective-permute-done.8
  147.2 5.3 %collective-permute-start.9 = (f32[54,128]{1,0:T(8,128)S(1)}, f32[54,128]{1,0:T(8,128)S(1)}, u32[]{:S(2)}, u32[]{:S(2)}) collective-permute-start(f32[54,128]{1,0:T(8,128)S(1)} %add.88), channel_id=1, source_target_pairs={{0,64},{1,65},{2,66},{3,67},{32,96},{33,97},{34,98},{35,99},{64,0}... | collective-permute-start | bytes 82952 | tf_op jit(solution)/shard_map/ppermute | solution.py:42
  152.6 1.8 %collective-permute-done.9 = f32[54,128]{1,0:T(8,128)S(1)} collective-permute-done((f32[54,128]{1,0:T(8,128)S(1)}, f32[54,128]{1,0:T(8,128)S(1)}, u32[]{:S(2)}, u32[]{:S(2)}) %collective-permute-start.9) | collective-permute-done | bytes 27680 | tf_op jit(solution)/shard_map/ppermute | solution.py:42
  155.0 7.0 %collective-permute-start.10 = (f32[54,128]{1,0:T(8,128)}, f32[54,128]{1,0:T(8,128)}, u32[]{:S(2)}, u32[]{:S(2)}) collective-permute-start(f32[54,128]{1,0:T(8,128)} %add.89), channel_id=1, source_target_pairs={{0,192},{1,193},{2,194},{3,195},{32,224},{33,225},{34,226},{35,227... | collective-permute-start | bytes 82952 | tf_op jit(solution)/shard_map/ppermute | solution.py:42
  162.6 1.7 reduce_sum.28
  164.3 0.8 add.90
  165.1 3.4 %collective-permute-start.11 = (f32[54,128]{1,0:T(8,128)S(1)}, f32[54,128]{1,0:T(8,128)S(1)}, u32[]{:S(2)}, u32[]{:S(2)}) collective-permute-start(f32[54,128]{1,0:T(8,128)S(1)} %add.90), channel_id=1, source_target_pairs={{0,256},{1,257},{2,258},{3,259},{32,288},{33,289},{34,290},{35,291... | collective-permute-start | bytes 82952 | tf_op jit(solution)/shard_map/ppermute | solution.py:42
  168.5 1.0 bitcast_add_fusion
  169.5 4.6 %collective-permute-start.16 = (f32[1,2,2,32,256]{4,3,2,1,0:T(8,128)S(1)}, f32[1,2,2,32,256]{4,3,2,1,0:T(8,128)S(1)}, u32[]{:S(2)}, u32[]{:S(2)}) collective-permute-start(f32[1,2,2,32,256]{4,3,2,1,0:T(8,128)S(1)} %dynamic-slice_bitcast_fusion.1), channel_id=1, source_target_pairs={{0,16},{4,20},{8,24},{12,28},{16,0},{20,4},{24,8},{28,12},{1,17},{... | collective-permute-start | bytes 393224 | tf_op jit(solution)/shard_map/ppermute | solution.py:128
  175.6 6.1 %collective-permute-done.16 = f32[1,2,2,32,256]{4,3,2,1,0:T(8,128)S(1)} collective-permute-done((f32[1,2,2,32,256]{4,3,2,1,0:T(8,128)S(1)}, f32[1,2,2,32,256]{4,3,2,1,0:T(8,128)S(1)}, u32[]{:S(2)}, u32[]{:S(2)}) %collective-permute-start.16) | collective-permute-done | bytes 131104 | tf_op jit(solution)/shard_map/ppermute | solution.py:128
  (90 shorter events, 16.0 us)
Async XLA Ops:
  1.4 3.0 %collective-permute-start = (bf16[1,4,1,4,512]{4,3,2,1,0:T(4,128)(2,1)S(1)}, bf16[1,4,1,4,512]{4,3,2,1,0:T(4,128)(2,1)S(1)}, u32[]{:S(2)}, u32[]{:S(2)}) collective-permute-start(bf16[1,4,1,4,512]{4,3,2,1,0:T(4,128)(2,1)S(1)} %get-tuple-element.60), channel_id=1, source_target_pairs={{0,32},{32,64},{64,96},{96,128},{128,160},{160,192},{192,224},{224... | collective-permute-start | bytes 49160 | tf_op jit(solution)/shard_map/ppermute | solution.py:15
  3.1 4.4 %collective-permute-start.1 = (bf16[1,4,1,4,512]{4,3,2,1,0:T(4,128)(2,1)S(1)}, bf16[1,4,1,4,512]{4,3,2,1,0:T(4,128)(2,1)S(1)}, u32[]{:S(2)}, u32[]{:S(2)}) collective-permute-start(bf16[1,4,1,4,512]{4,3,2,1,0:T(4,128)(2,1)S(1)} %get-tuple-element.59), channel_id=1, source_target_pairs={{32,0},{64,32},{96,64},{128,96},{160,128},{192,160},{224,192},{256... | collective-permute-start | bytes 49160 | tf_op jit(solution)/shard_map/ppermute | solution.py:18
  7.6 8.8 %collective-permute-start.2 = (bf16[1,4,6,1,512]{4,3,2,1,0:T(2,128)(2,1)S(1)}, bf16[1,4,6,1,512]{4,3,2,1,0:T(2,128)(2,1)S(1)}, u32[]{:S(2)}, u32[]{:S(2)}) collective-permute-start(bf16[1,4,6,1,512]{4,3,2,1,0:T(2,128)(2,1)S(1)} %get-tuple-element.57), channel_id=1, source_target_pairs={{0,4},{4,8},{8,12},{12,16},{16,20},{20,24},{24,28},{1,5},{5,9},{9,... | collective-permute-start | bytes 73736 | tf_op jit(solution)/shard_map/ppermute | solution.py:15
  11.1 6.0 %collective-permute-start.3 = (bf16[1,4,6,1,512]{4,3,2,1,0:T(2,128)(2,1)S(1)}, bf16[1,4,6,1,512]{4,3,2,1,0:T(2,128)(2,1)S(1)}, u32[]{:S(2)}, u32[]{:S(2)}) collective-permute-start(bf16[1,4,6,1,512]{4,3,2,1,0:T(2,128)(2,1)S(1)} %get-tuple-element.58), channel_id=1, source_target_pairs={{4,0},{8,4},{12,8},{16,12},{20,16},{24,20},{28,24},{5,1},{9,5},{13... | collective-permute-start | bytes 73736 | tf_op jit(solution)/shard_map/ppermute | solution.py:18
  35.1 0.7 copy-start.1
  45.3 31.0 %copy-start.3 = (bf16[8,864]{1,0:T(8,128)(2,1)S(1)}, bf16[8,864]{1,0:T(8,128)(2,1)}, u32[]{:S(2)}) copy-start(bf16[8,864]{1,0:T(8,128)(2,1)} %param.6) | copy-start | bytes 41476
  45.3 32.8 %copy-start.2 = (bf16[1,8,1,1024]{3,1,2,0:T(8,128)(2,1)S(1)}, bf16[1,8,1,1024]{3,1,2,0:T(8,128)(2,1)}, u32[]{:S(2)}) copy-start(bf16[1,8,1,1024]{3,1,2,0:T(8,128)(2,1)} %param.7) | copy-start | bytes 49156
  73.5 5.6 %collective-permute-start.4 = (bf16[1,32,1,16,256]{4,1,3,2,0:T(8,128)(2,1)S(1)}, bf16[1,32,1,16,256]{4,1,3,2,0:T(8,128)(2,1)S(1)}, u32[]{:S(2)}, u32[]{:S(2)}) collective-permute-start(bf16[1,32,1,16,256]{4,1,3,2,0:T(8,128)(2,1)S(1)} %get-tuple-element.41), channel_id=1, source_target_pairs={{0,32},{32,64},{64,96},{96,128},{128,160},{160,192},{192,224},{224... | collective-permute-start | bytes 786440 | tf_op jit(solution)/shard_map/ppermute | solution.py:15
  74.8 6.0 %collective-permute-start.5 = (bf16[1,32,1,16,256]{4,1,3,2,0:T(8,128)(2,1)S(1)}, bf16[1,32,1,16,256]{4,1,3,2,0:T(8,128)(2,1)S(1)}, u32[]{:S(2)}, u32[]{:S(2)}) collective-permute-start(bf16[1,32,1,16,256]{4,1,3,2,0:T(8,128)(2,1)S(1)} %get-tuple-element.42), channel_id=1, source_target_pairs={{32,0},{64,32},{96,64},{128,96},{160,128},{192,160},{224,192},{256... | collective-permute-start | bytes 786440 | tf_op jit(solution)/shard_map/ppermute | solution.py:18
  83.8 2.8 %copy-start = (bf16[8,3,32,3,3]{2,0,4,3,1:T(8,128)(2,1)S(1)}, bf16[8,3,32,3,3]{2,0,4,3,1:T(8,128)(2,1)}, u32[]{:S(2)}) copy-start(bf16[8,3,32,3,3]{2,0,4,3,1:T(8,128)(2,1)} %copy.405) | copy-start | bytes 41476
  89.3 8.2 %collective-permute-start.12 = (bf16[1,8,1,16,256]{4,1,3,2,0:T(8,128)(2,1)S(1)}, bf16[1,8,1,16,256]{4,1,3,2,0:T(8,128)(2,1)S(1)}, u32[]{:S(2)}, u32[]{:S(2)}) collective-permute-start(bf16[1,8,1,16,256]{4,1,3,2,0:T(8,128)(2,1)S(1)} %get-tuple-element.55), channel_id=1, source_target_pairs={{0,32},{32,64},{64,96},{96,128},{128,160},{160,192},{192,224},{224... | collective-permute-start | bytes 196616 | tf_op jit(solution)/shard_map/ppermute | solution.py:15
  96.0 3.1 %collective-permute-start.13 = (bf16[1,8,1,16,256]{4,1,3,2,0:T(8,128)(2,1)S(1)}, bf16[1,8,1,16,256]{4,1,3,2,0:T(8,128)(2,1)S(1)}, u32[]{:S(2)}, u32[]{:S(2)}) collective-permute-start(bf16[1,8,1,16,256]{4,1,3,2,0:T(8,128)(2,1)S(1)} %get-tuple-element.56), channel_id=1, source_target_pairs={{32,0},{64,32},{96,64},{128,96},{160,128},{192,160},{224,192},{256... | collective-permute-start | bytes 196616 | tf_op jit(solution)/shard_map/ppermute | solution.py:18
  101.6 15.0 %collective-permute-start.14 = (f32[2,2,1,2,2,32,256]{6,5,4,3,0,2,1:T(8,128)S(1)}, f32[2,2,1,2,2,32,256]{6,5,4,3,0,2,1:T(8,128)S(1)}, u32[]{:S(2)}, u32[]{:S(2)}) collective-permute-start(f32[2,2,1,2,2,32,256]{6,5,4,3,0,2,1:T(8,128)S(1)} %copy.444), channel_id=1, source_target_pairs={{0,4},{4,0},{8,12},{12,8},{16,20},{20,16},{24,28},{28,24},{1,5},{5... | collective-permute-start | bytes 1572872 | tf_op jit(solution)/shard_map/ppermute | solution.py:128
  116.7 51.9 %collective-permute-start.15 = (f32[2,1,2,2,32,256]{5,4,3,2,0,1:T(8,128)S(1)}, f32[2,1,2,2,32,256]{5,4,3,2,0,1:T(8,128)}, u32[]{:S(2)}, u32[]{:S(2)}) collective-permute-start(f32[2,1,2,2,32,256]{5,4,3,2,0,1:T(8,128)S(1)} %dynamic-slice_bitcast_fusion), channel_id=1, source_target_pairs={{0,8},{4,12},{8,0},{12,4},{16,24},{20,28},{24,16},{28,20},{1,9},{5... | collective-permute-start | bytes 786440 | tf_op jit(solution)/shard_map/ppermute | solution.py:128
  124.7 7.9 %collective-permute-start.6 = (f32[54,128]{1,0:T(8,128)S(1)}, f32[54,128]{1,0:T(8,128)S(1)}, u32[]{:S(2)}, u32[]{:S(2)}) collective-permute-start(f32[54,128]{1,0:T(8,128)S(1)} %mul.80), channel_id=1, source_target_pairs={{0,1},{1,0},{2,3},{3,2},{32,33},{33,32},{34,35},{35,34},{64,65},{6... | collective-permute-start | bytes 82952 | tf_op jit(solution)/shard_map/ppermute | solution.py:42
  132.6 11.5 %collective-permute-start.7 = (f32[54,128]{1,0:T(8,128)S(1)}, f32[54,128]{1,0:T(8,128)S(1)}, u32[]{:S(2)}, u32[]{:S(2)}) collective-permute-start(f32[54,128]{1,0:T(8,128)S(1)} %add.86), channel_id=1, source_target_pairs={{0,3},{1,2},{2,1},{3,0},{32,35},{33,34},{34,33},{35,32},{64,67},{6... | collective-permute-start | bytes 82952 | tf_op jit(solution)/shard_map/ppermute | solution.py:42
  144.1 3.1 %collective-permute-start.8 = (f32[54,128]{1,0:T(8,128)S(1)}, f32[54,128]{1,0:T(8,128)S(1)}, u32[]{:S(2)}, u32[]{:S(2)}) collective-permute-start(f32[54,128]{1,0:T(8,128)S(1)} %add.87), channel_id=1, source_target_pairs={{0,32},{1,33},{2,34},{3,35},{32,0},{33,1},{34,2},{35,3},{64,96},{6... | collective-permute-start | bytes 82952 | tf_op jit(solution)/shard_map/ppermute | solution.py:42
  147.2 7.2 %collective-permute-start.9 = (f32[54,128]{1,0:T(8,128)S(1)}, f32[54,128]{1,0:T(8,128)S(1)}, u32[]{:S(2)}, u32[]{:S(2)}) collective-permute-start(f32[54,128]{1,0:T(8,128)S(1)} %add.88), channel_id=1, source_target_pairs={{0,64},{1,65},{2,66},{3,67},{32,96},{33,97},{34,98},{35,99},{64,0}... | collective-permute-start | bytes 82952 | tf_op jit(solution)/shard_map/ppermute | solution.py:42
  155.0 9.3 %collective-permute-start.10 = (f32[54,128]{1,0:T(8,128)}, f32[54,128]{1,0:T(8,128)}, u32[]{:S(2)}, u32[]{:S(2)}) collective-permute-start(f32[54,128]{1,0:T(8,128)} %add.89), channel_id=1, source_target_pairs={{0,192},{1,193},{2,194},{3,195},{32,224},{33,225},{34,226},{35,227... | collective-permute-start | bytes 82952 | tf_op jit(solution)/shard_map/ppermute | solution.py:42
  165.1 9.8 %collective-permute-start.11 = (f32[54,128]{1,0:T(8,128)S(1)}, f32[54,128]{1,0:T(8,128)S(1)}, u32[]{:S(2)}, u32[]{:S(2)}) collective-permute-start(f32[54,128]{1,0:T(8,128)S(1)} %add.90), channel_id=1, source_target_pairs={{0,256},{1,257},{2,258},{3,259},{32,288},{33,289},{34,290},{35,291... | collective-permute-start | bytes 82952 | tf_op jit(solution)/shard_map/ppermute | solution.py:42
  169.5 12.1 %collective-permute-start.16 = (f32[1,2,2,32,256]{4,3,2,1,0:T(8,128)S(1)}, f32[1,2,2,32,256]{4,3,2,1,0:T(8,128)S(1)}, u32[]{:S(2)}, u32[]{:S(2)}) collective-permute-start(f32[1,2,2,32,256]{4,3,2,1,0:T(8,128)S(1)} %dynamic-slice_bitcast_fusion.1), channel_id=1, source_target_pairs={{0,16},{4,20},{8,24},{12,28},{16,0},{20,4},{24,8},{28,12},{1,17},{... | collective-permute-start | bytes 393224 | tf_op jit(solution)/shard_map/ppermute | solution.py:128
where the time goes:
time: 184 us; the launch traced here: 182 us
  starting transfers between devices  65.5 us (36%)
  local copies, waits for them, and re-layouts  39.8 us (22%)
  waiting for transfers between devices  31.5 us (17%)
  blocking collectives  27.9 us (15%)
  other arithmetic  10.1 us (5%)
  matrix products  6.18 us (3%)
    ppermute x6, starting transfers between devices, butterfly_sum(): values = values + lax.ppermute(values, axes, pairs)  33.4 us
    all_gather x1, blocking collectives, shards(): slab_rows = lax.all_gather(level_loc, 'height', axis=3, tiled=True)  27.9 us
    ppermute x3, waiting for transfers between devices, near_first_scatter(): grid = jnp.squeeze(keep + lax.ppermute(send, axis, pairs), axis_pos)  18.7 us
    another operation x14, local copies, waits for them, and re-layouts, delta_shifts(): jnp.stack([dpad[:, :, 2 - kh:2 - kh + hsize, 2 - kw:2 - kw + wsize] for k...  18.5 us
    ppermute x4, starting transfers between devices, extended(): lax.ppermute(lax.slice_in_dim(block, block.shape[dim] - width, None, axis...  13.2 us
    ppermute x3, starting transfers between devices, near_first_scatter(): grid = jnp.squeeze(keep + lax.ppermute(send, axis, pairs), axis_pos)  11.1 us
    ppermute x4, starting transfers between devices, extended(): lax.ppermute(lax.slice_in_dim(block, 0, width, axis=dim), axis, backward)  7.84 us
    unnamed x37, local copies, waits for them, and re-layouts  7.03 us
  transfers between devices with their start and end apart: 17, of which 10 were waited for; matrix products, arithmetic and copies ran while one was open for 8% of the time, Pallas kernels for 0%

commit v1 on v0

--- a/solution.py
+++ b/solution.py
@@ -186,7 +186,9 @@
     padded = extended(volume, (("depth", 2), ("height", 3)), 1)
     pre_one = forward_product(padded, first_kernel)[:, :, :, 1:-1]
     level_loc = pooled(activate(pre_one)).astype(jnp.bfloat16)
-    slab_rows = lax.all_gather(level_loc, "height", axis=3, tiled=True)
+    slab_rows = jnp.concatenate(
+        lax.all_to_all(jnp.stack([level_loc] * lax.axis_size("height")), "height", 0, 0), axis=3
+    )
     level_one = extended(slab_rows, (("depth", 2),), 1)
     pre_two = forward_product(level_one, second_kernel)
     pooled_grid = pooled(activate(pre_two)).astype(jnp.bfloat16)

time: 184 us -> 178 us (0.967)
  the two profiles are of different devices: /device:TPU:8 before, /device:TPU:16 now
where the time goes in v1:
time: 178 us; the launch traced here: 176 us
  starting transfers between devices  63.7 us (36%)
  local copies, waits for them, and re-layouts  39.9 us (22%)
  waiting for transfers between devices  32.6 us (18%)
  blocking collectives  22.5 us (13%)
  other arithmetic  10.1 us (6%)
  matrix products  6.18 us (3%)
    ppermute x6, starting transfers between devices, butterfly_sum(): values = values + lax.ppermute(values, axes, pairs)  33.4 us
    all_to_all x1, blocking collectives, shards(): lax.all_to_all(jnp.stack([level_loc] * lax.axis_size('height')), 'height'...  22.5 us
    ppermute x3, waiting for transfers between devices, near_first_scatter(): grid = jnp.squeeze(keep + lax.ppermute(send, axis, pairs), axis_pos)  18.8 us
    another operation x14, local copies, waits for them, and re-layouts, delta_shifts(): jnp.stack([dpad[:, :, 2 - kh:2 - kh + hsize, 2 - kw:2 - kw + wsize] for k...  18.5 us
    ppermute x4, starting transfers between devices, extended(): lax.ppermute(lax.slice_in_dim(block, block.shape[dim] - width, None, axis...  13.6 us
    ppermute x3, starting transfers between devices, near_first_scatter(): grid = jnp.squeeze(keep + lax.ppermute(send, axis, pairs), axis_pos)  10.3 us
    ppermute x4, waiting for transfers between devices, extended(): lax.ppermute(lax.slice_in_dim(block, 0, width, axis=dim), axis, backward)  7.08 us
    unnamed x37, local copies, waits for them, and re-layouts  7.03 us
  transfers between devices with their start and end apart: 17, of which 10 were waited for; matrix products, arithmetic and copies ran while one was open for 9% of the time, Pallas kernels for 0%

profile of v1, /device:TPU:16, one launch (start us, length us, event | category | flops | bytes accessed | tf_op | source)
XLA Modules:
  0.0 176.3 jit_solution(18061890987847699139)
XLA Ops:
  1.4 1.7 collective-permute-start
  3.1 1.3 collective-permute-start.1
  4.5 0.9 constant_dynamic-update-slice_fusion.1
  5.3 2.2 %collective-permute-done.1 = bf16[1,4,1,4,512]{4,3,2,1,0:T(4,128)(2,1)S(1)} collective-permute-done((bf16[1,4,1,4,512]{4,3,2,1,0:T(4,128)(2,1)S(1)}, bf16[1,4,1,4,512]{4,3,2,1,0:T(4,128)(2,1)S(1)}, u32[]{:S(2)}, u32[]{:S(2)}) %collective-permute-start.1) | collective-permute-done | bytes 16416 | tf_op jit(solution)/shard_map/ppermute | solution.py:18
  7.6 3.5 %collective-permute-start.2 = (bf16[1,4,6,1,512]{4,3,2,1,0:T(2,128)(2,1)S(1)}, bf16[1,4,6,1,512]{4,3,2,1,0:T(2,128)(2,1)S(1)}, u32[]{:S(2)}, u32[]{:S(2)}) collective-permute-start(bf16[1,4,6,1,512]{4,3,2,1,0:T(2,128)(2,1)S(1)} %get-tuple-element.60), channel_id=1, source_target_pairs={{0,4},{4,8},{8,12},{12,16},{16,20},{20,24},{24,28},{1,5},{5,9},{9,... | collective-permute-start | bytes 73736 | tf_op jit(solution)/shard_map/ppermute | solution.py:15
  11.1 2.4 %collective-permute-start.3 = (bf16[1,4,6,1,512]{4,3,2,1,0:T(2,128)(2,1)S(1)}, bf16[1,4,6,1,512]{4,3,2,1,0:T(2,128)(2,1)S(1)}, u32[]{:S(2)}, u32[]{:S(2)}) collective-permute-start(bf16[1,4,6,1,512]{4,3,2,1,0:T(2,128)(2,1)S(1)} %get-tuple-element.61), channel_id=1, source_target_pairs={{4,0},{8,4},{12,8},{16,12},{20,16},{24,20},{28,24},{5,1},{9,5},{13... | collective-permute-start | bytes 73736 | tf_op jit(solution)/shard_map/ppermute | solution.py:18
  13.4 0.8 copy.436
  15.0 2.8 %collective-permute-done.3 = bf16[1,4,6,1,512]{4,3,2,1,0:T(2,128)(2,1)S(1)} collective-permute-done((bf16[1,4,6,1,512]{4,3,2,1,0:T(2,128)(2,1)S(1)}, bf16[1,4,6,1,512]{4,3,2,1,0:T(2,128)(2,1)S(1)}, u32[]{:S(2)}, u32[]{:S(2)}) %collective-permute-start.3) | collective-permute-done | bytes 24608 | tf_op jit(solution)/shard_map/ppermute | solution.py:18
  19.7 0.9 copy.430
  20.6 0.9 copy.431
  21.6 1.0 copy.432
  22.6 0.9 copy.433
  23.5 0.9 copy.429
  24.4 11.4 %stack.179 = bf16[4,9,6,6,512]{4,1,0,3,2:T(8,128)(2,1)S(1)} concatenate(bf16[4,1,6,6,512]{4,1,0,3,2:T(2,128)(2,1)S(1)} %copy.425, bf16[4,1,6,6,512]{4,1,0,3,2:T(2,128)(2,1)S(1)} %copy.426, bf16[4,1,6,6,512]{4,1,0,3,2:T(2,128)(2,1)S(1)} %copy.427, bf16[4,1,6,6,512]{4,1,0,3,2:T(2,128)(2,1)S(1)} %copy.428, bf16[4,1,6,6,512]{4,1,0,3,2:T(2,128)(2,1)} %copy.429, ...), dimensions={1} | concatenate | bytes 2654208 | tf_op jit(solution)/shard_map/stack | solution.py:67
  36.6 1.4 fusion.27
  38.7 2.6 %copy.439 = f32[1,32,4,4,512]{1,4,3,2,0:T(8,128)} copy(f32[1,32,4,4,512]{4,1,3,2,0:T(8,128)S(1)} %fusion.61) | data formatting | bytes 2097152 | tf_op jit(solution)/shard_map/add | solution.py:133
  41.3 4.8 %reduce_sum.21 = f32[32,2,2,256]{0,3,2,1:T(8,128)S(1)} reduce(f32[32,2,2,2,2,256,2]{0,6,5,4,3,2,1:T(2,128)} %bitcast.267, f32[]{:T(128)} %constant.17.clone.1), dimensions={2,4,6}, to_apply=%region_0.1 | reduce | flops 229376 | bytes 1179652 | tf_op jit(solution)/shard_map/reduce_sum | solution.py:143
  46.4 22.5 %all_to_all.5 = bf16[8,1,32,2,2,256]{5,2,4,3,1,0:T(8,128)(2,1)S(1)} all-to-all(bf16[8,1,32,2,2,256]{5,2,4,3,1,0:T(8,128)(2,1)S(1)} %stack.184), channel_id=1, replica_groups=mesh['depth'=16,'height'=8,'sample'=4] {'height'}, dimensions={0} | all-to-all | bytes 1048576 | tf_op jit(solution)/shard_map/all_to_all | solution.py:190
  68.9 1.7 collective-permute-start.4
  70.6 1.5 collective-permute-start.5
  73.2 0.8 copy.453
  78.4 2.8 %slice_bitcast_fusion.2 = (bf16[1,32,9,2,16,256]{5,1,2,0,4,3:T(8,128)(2,1)S(1)}, bf16[1,32,9,2,16,256]{5,1,2,0,4,3:T(8,128)(2,1)S(1)}, bf16[1,32,9,2,16,256]{5,1,2,0,4,3:T(8,128)(2,1)S(1)}) fusion(bf16[32,9,4,16,256]{4,0,1,3,2:T(8,128)(2,1)S(1)} %fusion.59), kind=kLoop, calls=%fused_computation.8 | loop fusion | bytes 28311552 | tf_op jit(solution)/shard_map/stack | solution.py:103
  81.2 2.6 %multiply_convert_fusion.1 = (bf16[8,2,16,256]{3,0,2,1:T(8,128)(2,1)S(1)}, f32[8,16,256]{2,0,1:T(8,128)S(1)}) fusion(f32[8,16,256]{2,0,1:T(8,128)S(1)} %copy.456, bf16[8,3,32,9,1,1]{2,0,3,1,5,4:T(8,128)(2,1)S(1)} %bitcast.283, bf16[1,32,9,2,16,256]{5,1,2,0,4,3:T(8,128)(2,1)S(1)} %get-tuple-element.34, ...), kind=kOutput, calls=%fused_computation.113 | convolution fusion | flops 128483328 | bytes 14562816 | tf_op jit(solution)/shard_map/dot_general | solution.py:106
  83.9 6.7 %collective-permute-start.12 = (bf16[1,8,1,16,256]{4,1,3,2,0:T(8,128)(2,1)S(1)}, bf16[1,8,1,16,256]{4,1,3,2,0:T(8,128)(2,1)S(1)}, u32[]{:S(2)}, u32[]{:S(2)}) collective-permute-start(bf16[1,8,1,16,256]{4,1,3,2,0:T(8,128)(2,1)S(1)} %get-tuple-element.58), channel_id=1, source_target_pairs={{0,32},{32,64},{64,96},{96,128},{128,160},{160,192},{192,224},{224... | collective-permute-start | bytes 196616 | tf_op jit(solution)/shard_map/ppermute | solution.py:15
  90.6 1.3 collective-permute-start.13
  92.2 1.6 collective-permute-done.13
  95.1 0.9 fusion.12
  96.2 2.8 %collective-permute-start.14 = (f32[2,2,1,2,2,32,256]{6,5,4,3,0,2,1:T(8,128)S(1)}, f32[2,2,1,2,2,32,256]{6,5,4,3,0,2,1:T(8,128)S(1)}, u32[]{:S(2)}, u32[]{:S(2)}) collective-permute-start(f32[2,2,1,2,2,32,256]{6,5,4,3,0,2,1:T(8,128)S(1)} %copy.492), channel_id=1, source_target_pairs={{0,4},{4,0},{8,12},{12,8},{16,20},{20,16},{24,28},{28,24},{1,5},{5... | collective-permute-start | bytes 1572872 | tf_op jit(solution)/shard_map/ppermute | solution.py:128
  99.4 11.9 %collective-permute-done.14 = f32[2,2,1,2,2,32,256]{6,5,4,3,0,2,1:T(8,128)S(1)} collective-permute-done((f32[2,2,1,2,2,32,256]{6,5,4,3,0,2,1:T(8,128)S(1)}, f32[2,2,1,2,2,32,256]{6,5,4,3,0,2,1:T(8,128)S(1)}, u32[]{:S(2)}, u32[]{:S(2)}) %collective-permute-start.14) | collective-permute-done | bytes 524320 | tf_op jit(solution)/shard_map/ppermute | solution.py:128
  111.4 5.0 %collective-permute-start.15 = (f32[2,1,2,2,32,256]{5,4,3,2,0,1:T(8,128)S(1)}, f32[2,1,2,2,32,256]{5,4,3,2,0,1:T(8,128)}, u32[]{:S(2)}, u32[]{:S(2)}) collective-permute-start(f32[2,1,2,2,32,256]{5,4,3,2,0,1:T(8,128)S(1)} %dynamic-slice_bitcast_fusion), channel_id=1, source_target_pairs={{0,8},{4,12},{8,0},{12,4},{16,24},{20,28},{24,16},{28,20},{1,9},{5... | collective-permute-start | bytes 786440 | tf_op jit(solution)/shard_map/ppermute | solution.py:128
  116.4 1.2 fusion.39
  117.6 1.2 copy.457
  118.8 1.0 mul.80
  119.8 6.1 %collective-permute-start.6 = (f32[54,128]{1,0:T(8,128)S(1)}, f32[54,128]{1,0:T(8,128)S(1)}, u32[]{:S(2)}, u32[]{:S(2)}) collective-permute-start(f32[54,128]{1,0:T(8,128)S(1)} %mul.80), channel_id=1, source_target_pairs={{0,1},{1,0},{2,3},{3,2},{32,33},{33,32},{34,35},{35,34},{64,65},{6... | collective-permute-start | bytes 82952 | tf_op jit(solution)/shard_map/ppermute | solution.py:42
  125.9 1.8 %collective-permute-done.6 = f32[54,128]{1,0:T(8,128)S(1)} collective-permute-done((f32[54,128]{1,0:T(8,128)S(1)}, f32[54,128]{1,0:T(8,128)S(1)}, u32[]{:S(2)}, u32[]{:S(2)}) %collective-permute-start.6) | collective-permute-done | bytes 27680 | tf_op jit(solution)/shard_map/ppermute | solution.py:42
  127.7 9.8 %collective-permute-start.7 = (f32[54,128]{1,0:T(8,128)S(1)}, f32[54,128]{1,0:T(8,128)S(1)}, u32[]{:S(2)}, u32[]{:S(2)}) collective-permute-start(f32[54,128]{1,0:T(8,128)S(1)} %add.86), channel_id=1, source_target_pairs={{0,3},{1,2},{2,1},{3,0},{32,35},{33,34},{34,33},{35,32},{64,67},{6... | collective-permute-start | bytes 82952 | tf_op jit(solution)/shard_map/ppermute | solution.py:42
  137.5 1.8 %collective-permute-done.7 = f32[54,128]{1,0:T(8,128)S(1)} collective-permute-done((f32[54,128]{1,0:T(8,128)S(1)}, f32[54,128]{1,0:T(8,128)S(1)}, u32[]{:S(2)}, u32[]{:S(2)}) %collective-permute-start.7) | collective-permute-done | bytes 27680 | tf_op jit(solution)/shard_map/ppermute | solution.py:42
  139.4 1.9 %collective-permute-start.8 = (f32[54,128]{1,0:T(8,128)S(1)}, f32[54,128]{1,0:T(8,128)S(1)}, u32[]{:S(2)}, u32[]{:S(2)}) collective-permute-start(f32[54,128]{1,0:T(8,128)S(1)} %add.87), channel_id=1, source_target_pairs={{0,32},{1,33},{2,34},{3,35},{32,0},{33,1},{34,2},{35,3},{64,96},{6... | collective-permute-start | bytes 82952 | tf_op jit(solution)/shard_map/ppermute | solution.py:42
  141.3 1.2 collective-permute-done.8
  142.5 5.0 %collective-permute-start.9 = (f32[54,128]{1,0:T(8,128)S(1)}, f32[54,128]{1,0:T(8,128)S(1)}, u32[]{:S(2)}, u32[]{:S(2)}) collective-permute-start(f32[54,128]{1,0:T(8,128)S(1)} %add.88), channel_id=1, source_target_pairs={{0,64},{1,65},{2,66},{3,67},{32,96},{33,97},{34,98},{35,99},{64,0}... | collective-permute-start | bytes 82952 | tf_op jit(solution)/shard_map/ppermute | solution.py:42
  147.5 1.8 %collective-permute-done.9 = f32[54,128]{1,0:T(8,128)S(1)} collective-permute-done((f32[54,128]{1,0:T(8,128)S(1)}, f32[54,128]{1,0:T(8,128)S(1)}, u32[]{:S(2)}, u32[]{:S(2)}) %collective-permute-start.9) | collective-permute-done | bytes 27680 | tf_op jit(solution)/shard_map/ppermute | solution.py:42
  149.9 4.9 %collective-permute-start.10 = (f32[54,128]{1,0:T(8,128)}, f32[54,128]{1,0:T(8,128)}, u32[]{:S(2)}, u32[]{:S(2)}) collective-permute-start(f32[54,128]{1,0:T(8,128)} %add.89), channel_id=1, source_target_pairs={{0,192},{1,193},{2,194},{3,195},{32,224},{33,225},{34,226},{35,227... | collective-permute-start | bytes 82952 | tf_op jit(solution)/shard_map/ppermute | solution.py:42
  155.5 1.7 reduce_sum.28
  157.2 0.8 add.90
  158.0 5.7 %collective-permute-start.11 = (f32[54,128]{1,0:T(8,128)S(1)}, f32[54,128]{1,0:T(8,128)S(1)}, u32[]{:S(2)}, u32[]{:S(2)}) collective-permute-start(f32[54,128]{1,0:T(8,128)S(1)} %add.90), channel_id=1, source_target_pairs={{0,256},{1,257},{2,258},{3,259},{32,288},{33,289},{34,290},{35,291... | collective-permute-start | bytes 82952 | tf_op jit(solution)/shard_map/ppermute | solution.py:42
  163.6 1.0 bitcast_add_fusion
  164.7 2.5 %collective-permute-start.16 = (f32[1,2,2,32,256]{4,3,2,1,0:T(8,128)S(1)}, f32[1,2,2,32,256]{4,3,2,1,0:T(8,128)S(1)}, u32[]{:S(2)}, u32[]{:S(2)}) collective-permute-start(f32[1,2,2,32,256]{4,3,2,1,0:T(8,128)S(1)} %dynamic-slice_bitcast_fusion.1), channel_id=1, source_target_pairs={{0,16},{4,20},{8,24},{12,28},{16,0},{20,4},{24,8},{28,12},{1,17},{... | collective-permute-start | bytes 393224 | tf_op jit(solution)/shard_map/ppermute | solution.py:128
  168.6 6.9 %collective-permute-done.16 = f32[1,2,2,32,256]{4,3,2,1,0:T(8,128)S(1)} collective-permute-done((f32[1,2,2,32,256]{4,3,2,1,0:T(8,128)S(1)}, f32[1,2,2,32,256]{4,3,2,1,0:T(8,128)S(1)}, u32[]{:S(2)}, u32[]{:S(2)}) %collective-permute-start.16) | collective-permute-done | bytes 131104 | tf_op jit(solution)/shard_map/ppermute | solution.py:128
  (92 shorter events, 16.0 us)
Async XLA Ops:
  1.4 3.0 %collective-permute-start = (bf16[1,4,1,4,512]{4,3,2,1,0:T(4,128)(2,1)S(1)}, bf16[1,4,1,4,512]{4,3,2,1,0:T(4,128)(2,1)S(1)}, u32[]{:S(2)}, u32[]{:S(2)}) collective-permute-start(bf16[1,4,1,4,512]{4,3,2,1,0:T(4,128)(2,1)S(1)} %get-tuple-element.63), channel_id=1, source_target_pairs={{0,32},{32,64},{64,96},{96,128},{128,160},{160,192},{192,224},{224... | collective-permute-start | bytes 49160 | tf_op jit(solution)/shard_map/ppermute | solution.py:15
  3.1 4.4 %collective-permute-start.1 = (bf16[1,4,1,4,512]{4,3,2,1,0:T(4,128)(2,1)S(1)}, bf16[1,4,1,4,512]{4,3,2,1,0:T(4,128)(2,1)S(1)}, u32[]{:S(2)}, u32[]{:S(2)}) collective-permute-start(bf16[1,4,1,4,512]{4,3,2,1,0:T(4,128)(2,1)S(1)} %get-tuple-element.62), channel_id=1, source_target_pairs={{32,0},{64,32},{96,64},{128,96},{160,128},{192,160},{224,192},{256... | collective-permute-start | bytes 49160 | tf_op jit(solution)/shard_map/ppermute | solution.py:18
  7.6 7.4 %collective-permute-start.2 = (bf16[1,4,6,1,512]{4,3,2,1,0:T(2,128)(2,1)S(1)}, bf16[1,4,6,1,512]{4,3,2,1,0:T(2,128)(2,1)S(1)}, u32[]{:S(2)}, u32[]{:S(2)}) collective-permute-start(bf16[1,4,6,1,512]{4,3,2,1,0:T(2,128)(2,1)S(1)} %get-tuple-element.60), channel_id=1, source_target_pairs={{0,4},{4,8},{8,12},{12,16},{16,20},{20,24},{24,28},{1,5},{5,9},{9,... | collective-permute-start | bytes 73736 | tf_op jit(solution)/shard_map/ppermute | solution.py:15
  11.1 6.8 %collective-permute-start.3 = (bf16[1,4,6,1,512]{4,3,2,1,0:T(2,128)(2,1)S(1)}, bf16[1,4,6,1,512]{4,3,2,1,0:T(2,128)(2,1)S(1)}, u32[]{:S(2)}, u32[]{:S(2)}) collective-permute-start(bf16[1,4,6,1,512]{4,3,2,1,0:T(2,128)(2,1)S(1)} %get-tuple-element.61), channel_id=1, source_target_pairs={{4,0},{8,4},{12,8},{16,12},{20,16},{24,20},{28,24},{5,1},{9,5},{13... | collective-permute-start | bytes 73736 | tf_op jit(solution)/shard_map/ppermute | solution.py:18
  35.9 0.7 copy-start.1
  46.1 26.1 %copy-start.3 = (bf16[8,864]{1,0:T(8,128)(2,1)S(1)}, bf16[8,864]{1,0:T(8,128)(2,1)}, u32[]{:S(2)}) copy-start(bf16[8,864]{1,0:T(8,128)(2,1)} %param.6) | copy-start | bytes 41476
  46.3 27.6 %copy-start.2 = (bf16[1,8,1,1024]{3,1,2,0:T(8,128)(2,1)S(1)}, bf16[1,8,1,1024]{3,1,2,0:T(8,128)(2,1)}, u32[]{:S(2)}) copy-start(bf16[1,8,1,1024]{3,1,2,0:T(8,128)(2,1)} %param.7) | copy-start | bytes 49156
  68.9 6.0 %collective-permute-start.4 = (bf16[1,32,1,16,256]{4,1,3,2,0:T(8,128)(2,1)S(1)}, bf16[1,32,1,16,256]{4,1,3,2,0:T(8,128)(2,1)S(1)}, u32[]{:S(2)}, u32[]{:S(2)}) collective-permute-start(bf16[1,32,1,16,256]{4,1,3,2,0:T(8,128)(2,1)S(1)} %get-tuple-element.44), channel_id=1, source_target_pairs={{0,32},{32,64},{64,96},{96,128},{128,160},{160,192},{192,224},{224... | collective-permute-start | bytes 786440 | tf_op jit(solution)/shard_map/ppermute | solution.py:15
  70.6 4.8 %collective-permute-start.5 = (bf16[1,32,1,16,256]{4,1,3,2,0:T(8,128)(2,1)S(1)}, bf16[1,32,1,16,256]{4,1,3,2,0:T(8,128)(2,1)S(1)}, u32[]{:S(2)}, u32[]{:S(2)}) collective-permute-start(bf16[1,32,1,16,256]{4,1,3,2,0:T(8,128)(2,1)S(1)} %get-tuple-element.45), channel_id=1, source_target_pairs={{32,0},{64,32},{96,64},{128,96},{160,128},{192,160},{224,192},{256... | collective-permute-start | bytes 786440 | tf_op jit(solution)/shard_map/ppermute | solution.py:18
  78.4 2.8 %copy-start = (bf16[8,3,32,3,3]{2,0,4,3,1:T(8,128)(2,1)S(1)}, bf16[8,3,32,3,3]{2,0,4,3,1:T(8,128)(2,1)}, u32[]{:S(2)}) copy-start(bf16[8,3,32,3,3]{2,0,4,3,1:T(8,128)(2,1)} %copy.453) | copy-start | bytes 41476
  83.9 8.2 %collective-permute-start.12 = (bf16[1,8,1,16,256]{4,1,3,2,0:T(8,128)(2,1)S(1)}, bf16[1,8,1,16,256]{4,1,3,2,0:T(8,128)(2,1)S(1)}, u32[]{:S(2)}, u32[]{:S(2)}) collective-permute-start(bf16[1,8,1,16,256]{4,1,3,2,0:T(8,128)(2,1)S(1)} %get-tuple-element.58), channel_id=1, source_target_pairs={{0,32},{32,64},{64,96},{96,128},{128,160},{160,192},{192,224},{224... | collective-permute-start | bytes 196616 | tf_op jit(solution)/shard_map/ppermute | solution.py:15
  90.6 3.1 %collective-permute-start.13 = (bf16[1,8,1,16,256]{4,1,3,2,0:T(8,128)(2,1)S(1)}, bf16[1,8,1,16,256]{4,1,3,2,0:T(8,128)(2,1)S(1)}, u32[]{:S(2)}, u32[]{:S(2)}) collective-permute-start(bf16[1,8,1,16,256]{4,1,3,2,0:T(8,128)(2,1)S(1)} %get-tuple-element.59), channel_id=1, source_target_pairs={{32,0},{64,32},{96,64},{128,96},{160,128},{192,160},{224,192},{256... | collective-permute-start | bytes 196616 | tf_op jit(solution)/shard_map/ppermute | solution.py:18
  96.2 15.1 %collective-permute-start.14 = (f32[2,2,1,2,2,32,256]{6,5,4,3,0,2,1:T(8,128)S(1)}, f32[2,2,1,2,2,32,256]{6,5,4,3,0,2,1:T(8,128)S(1)}, u32[]{:S(2)}, u32[]{:S(2)}) collective-permute-start(f32[2,2,1,2,2,32,256]{6,5,4,3,0,2,1:T(8,128)S(1)} %copy.492), channel_id=1, source_target_pairs={{0,4},{4,0},{8,12},{12,8},{16,20},{20,16},{24,28},{28,24},{1,5},{5... | collective-permute-start | bytes 1572872 | tf_op jit(solution)/shard_map/ppermute | solution.py:128
  111.4 52.2 %collective-permute-start.15 = (f32[2,1,2,2,32,256]{5,4,3,2,0,1:T(8,128)S(1)}, f32[2,1,2,2,32,256]{5,4,3,2,0,1:T(8,128)}, u32[]{:S(2)}, u32[]{:S(2)}) collective-permute-start(f32[2,1,2,2,32,256]{5,4,3,2,0,1:T(8,128)S(1)} %dynamic-slice_bitcast_fusion), channel_id=1, source_target_pairs={{0,8},{4,12},{8,0},{12,4},{16,24},{20,28},{24,16},{28,20},{1,9},{5... | collective-permute-start | bytes 786440 | tf_op jit(solution)/shard_map/ppermute | solution.py:128
  119.8 7.9 %collective-permute-start.6 = (f32[54,128]{1,0:T(8,128)S(1)}, f32[54,128]{1,0:T(8,128)S(1)}, u32[]{:S(2)}, u32[]{:S(2)}) collective-permute-start(f32[54,128]{1,0:T(8,128)S(1)} %mul.80), channel_id=1, source_target_pairs={{0,1},{1,0},{2,3},{3,2},{32,33},{33,32},{34,35},{35,34},{64,65},{6... | collective-permute-start | bytes 82952 | tf_op jit(solution)/shard_map/ppermute | solution.py:42
  127.7 11.6 %collective-permute-start.7 = (f32[54,128]{1,0:T(8,128)S(1)}, f32[54,128]{1,0:T(8,128)S(1)}, u32[]{:S(2)}, u32[]{:S(2)}) collective-permute-start(f32[54,128]{1,0:T(8,128)S(1)} %add.86), channel_id=1, source_target_pairs={{0,3},{1,2},{2,1},{3,0},{32,35},{33,34},{34,33},{35,32},{64,67},{6... | collective-permute-start | bytes 82952 | tf_op jit(solution)/shard_map/ppermute | solution.py:42
  139.4 3.1 %collective-permute-start.8 = (f32[54,128]{1,0:T(8,128)S(1)}, f32[54,128]{1,0:T(8,128)S(1)}, u32[]{:S(2)}, u32[]{:S(2)}) collective-permute-start(f32[54,128]{1,0:T(8,128)S(1)} %add.87), channel_id=1, source_target_pairs={{0,32},{1,33},{2,34},{3,35},{32,0},{33,1},{34,2},{35,3},{64,96},{6... | collective-permute-start | bytes 82952 | tf_op jit(solution)/shard_map/ppermute | solution.py:42
  142.5 6.8 %collective-permute-start.9 = (f32[54,128]{1,0:T(8,128)S(1)}, f32[54,128]{1,0:T(8,128)S(1)}, u32[]{:S(2)}, u32[]{:S(2)}) collective-permute-start(f32[54,128]{1,0:T(8,128)S(1)} %add.88), channel_id=1, source_target_pairs={{0,64},{1,65},{2,66},{3,67},{32,96},{33,97},{34,98},{35,99},{64,0}... | collective-permute-start | bytes 82952 | tf_op jit(solution)/shard_map/ppermute | solution.py:42
  149.9 7.3 %collective-permute-start.10 = (f32[54,128]{1,0:T(8,128)}, f32[54,128]{1,0:T(8,128)}, u32[]{:S(2)}, u32[]{:S(2)}) collective-permute-start(f32[54,128]{1,0:T(8,128)} %add.89), channel_id=1, source_target_pairs={{0,192},{1,193},{2,194},{3,195},{32,224},{33,225},{34,226},{35,227... | collective-permute-start | bytes 82952 | tf_op jit(solution)/shard_map/ppermute | solution.py:42
  158.0 10.0 %collective-permute-start.11 = (f32[54,128]{1,0:T(8,128)S(1)}, f32[54,128]{1,0:T(8,128)S(1)}, u32[]{:S(2)}, u32[]{:S(2)}) collective-permute-start(f32[54,128]{1,0:T(8,128)S(1)} %add.90), channel_id=1, source_target_pairs={{0,256},{1,257},{2,258},{3,259},{32,288},{33,289},{34,290},{35,291... | collective-permute-start | bytes 82952 | tf_op jit(solution)/shard_map/ppermute | solution.py:42
  164.7 10.9 %collective-permute-start.16 = (f32[1,2,2,32,256]{4,3,2,1,0:T(8,128)S(1)}, f32[1,2,2,32,256]{4,3,2,1,0:T(8,128)S(1)}, u32[]{:S(2)}, u32[]{:S(2)}) collective-permute-start(f32[1,2,2,32,256]{4,3,2,1,0:T(8,128)S(1)} %dynamic-slice_bitcast_fusion.1), channel_id=1, source_target_pairs={{0,16},{4,20},{8,24},{12,28},{16,0},{20,4},{24,8},{28,12},{1,17},{... | collective-permute-start | bytes 393224 | tf_op jit(solution)/shard_map/ppermute | solution.py:128
